TPU v7x, 32 devices: a whole 2x2x4 slice. The times are simulated.
32 devices in a mesh: gx: 8 (over z, x), gy: 4 (over y, core).
Axes of the slice: x: 2, y: 2, z: 4, core: 2. Of those that a mesh axis runs over, the one named last changes fastest.
Arguments:
- prior_basis: float32 [128, 128, 128], P('gx', 'gy'), may hold values from -6 to 6
- cond_x: float32 [128, 128], P('gx', 'gy'), may hold values from 0.5 to 5
- cond_y: float32 [128, 128], P('gx', 'gy'), may hold values from 0.5 to 5
- capacitance: float32 [128, 128], P('gx', 'gy'), may hold values from 0.05 to 1
- pad_mask: int32 [128, 128], P('gx', 'gy'), may hold values 0 or 1
- port_nodes: int32 [128], replicated, may hold values from 0 to 16383
Outputs:
- new_basis: float32 [128, 128, 128], P('gx', 'gy')
- reduced_g: float32 [128, 128], replicated
- reduced_c: float32 [128, 128], replicated
Inputs may be any that keep to these rules, and one draw needn't show every extreme that they name: `port_nodes`: a row-major node index into the grid of 128 x 128 nodes.
All inputs are finite; a program needn't handle non-finite values. No bound on the sum of `pad_mask` on one device may be relied on, other than what follows from the above.
Results may differ from a plain program's by a relative error of at most 0.0003.
Values sent between devices are 32-bit elements; how exact they have to be, the bound alone decides.
No kernel may reach another device: no remote copies, remote signals or barrier semaphores. Data moves between devices by JAX's collectives and lax.ppermute only.
A program may use at most 64 MiB of HBM per device.

v0:
```python
import jax
import jax.numpy as jnp
from jax import lax
from jax.sharding import PartitionSpec as P

SWEEPS = 4
shift_point = 0.5
supply_conductance = 4.0
port_current = 8.0
highest = lax.Precision.HIGHEST


def shifted(shard, axis, by):
    devices = lax.axis_size(axis)
    pairs = [(i, i + by) for i in range(devices) if 0 <= i + by < devices]
    return lax.ppermute(shard, axis, pairs)


def padded(cells, sides, width):
    for axis, dim in sides:
        count = lax.axis_size(axis)
        ends = count - 1
        head = lax.slice_in_dim(cells, 0, width, axis=dim)
        tail = lax.slice_in_dim(cells, cells.shape[dim] - width, cells.shape[dim], axis=dim)
        cells = jnp.concatenate(
            [
                lax.ppermute(tail, axis, [(i, (i + 1) % count) for i in range(ends)]),
                cells,
                lax.ppermute(head, axis, [((i + 1) % count, i) for i in range(ends)]),
            ],
            axis=dim,
        )
    return cells


def neighbors(ext, links):
    cx, cy, cx_up, cy_left = links
    total = cx[:, :, None] * ext[2:, 1:-1] + cx_up[:, :, None] * ext[:-2, 1:-1]
    return total + cy[:, :, None] * ext[1:-1, 2:] + cy_left[:, :, None] * ext[1:-1, :-2]


def local_inner(left, right):
    a = left.reshape(-1, left.shape[-1])
    b = right.reshape(-1, right.shape[-1])
    return jnp.einsum("cp,cq->pq", a, b, precision=highest, preferred_element_type=jnp.float32)


def per_device(prior_basis, cond_x, cond_y, capacitance, pad_mask, port_nodes):
    rows_dev, cols_dev = cond_x.shape
    width = port_nodes.shape[0]
    count_x = lax.axis_size("gx")
    count_y = lax.axis_size("gy")
    total_rows = rows_dev * count_x
    total_cols = cols_dev * count_y
    nodes = total_rows * total_cols
    row_start = lax.axis_index("gx") * rows_dev
    col_start = lax.axis_index("gy") * cols_dev
    global_rows = row_start + jnp.arange(rows_dev, dtype=jnp.int32)[:, None]
    global_cols = col_start + jnp.arange(cols_dev, dtype=jnp.int32)[None, :]
    cx = jnp.where(global_rows < total_rows - 1, cond_x, jnp.float32(0.0))
    cy = jnp.where(global_cols < total_cols - 1, cond_y, jnp.float32(0.0))
    above = shifted(cx[-1:, :], "gx", 1)
    beside = shifted(cy[:, -1:], "gy", 1)
    cx_up = jnp.concatenate([above, cx[:-1]], axis=0)
    cy_left = jnp.concatenate([beside, cy[:, :-1]], axis=1)
    links = (cx, cy, cx_up, cy_left)
    diag_g = cx + cx_up + cy + cy_left + supply_conductance * pad_mask.astype(jnp.float32)
    diag = (diag_g + shift_point * capacitance)[:, :, None]
    node_ids = global_rows * total_cols + global_cols
    onehot = (node_ids[:, :, None] == port_nodes[None, None, :]).astype(jnp.float32)
    rhs = capacitance[:, :, None] * prior_basis + port_current * onehot

    def sweep(step, current):
        ext = padded(current, (("gx", 0), ("gy", 1)), 1)
        return (rhs + neighbors(ext, links)) / diag

    field = lax.fori_loop(0, SWEEPS, sweep, rhs / diag)
    proj = lax.psum(local_inner(prior_basis, field), ("gx", "gy")) / nodes
    cand = field - jnp.einsum("xyk,kp->xyp", prior_basis, proj, precision=highest)
    gram = lax.psum(local_inner(cand, cand), ("gx", "gy")) / nodes
    lower = jnp.linalg.cholesky(gram)
    flat = cand.reshape(-1, width)
    basis_flat = lax.linalg.triangular_solve(
        lower, flat, left_side=False, lower=True, transpose_a=True
    )
    new_basis = basis_flat.reshape(rows_dev, cols_dev, width)
    ext = padded(new_basis, (("gx", 0), ("gy", 1)), 1)
    g_image = diag_g[:, :, None] * new_basis - neighbors(ext, links)
    g_raw, c_raw = lax.psum(
        (
            local_inner(new_basis, g_image),
            local_inner(new_basis, capacitance[:, :, None] * new_basis),
        ),
        ("gx", "gy"),
    )
    reduced_g = g_raw / nodes
    reduced_c = c_raw / nodes
    return (new_basis, reduced_g, reduced_c)


def solution(mesh):
    placed = (P("gx", "gy", None), P("gx", "gy"), P("gx", "gy"), P("gx", "gy"), P("gx", "gy"), P())
    return jax.shard_map(
        per_device,
        mesh=mesh,
        in_specs=placed,
        out_specs=(P("gx", "gy", None), P(), P()),
        check_vma=False,
    )
```

profile of v0, /device:TPU:0, one launch (start us, length us, event | category | flops | bytes accessed | tf_op | source)
XLA Modules:
  0.0 506.1 jit_solution(9967310550308028480)
XLA Ops:
  7.9 2.5 collective-permute-start.5
  10.5 4.2 collective-permute-start.4
  14.9 1.2 collective-permute-done.4
  16.8 1.2 broadcast_divide_fusion
  18.0 68.9 %while.10 = (s32[]{:T(128)}, f32[16,32,128]{2,1,0:T(8,128)S(1)}, f32[16,32]{1,0:T(8,128)S(1)}, f32[16,32]{1,0:T(8,128)S(1)}, f32[16,32]{1,0:T(8,128)S(1)}, /*ind...) while((s32[]{:T(128)}, f32[16,32,128]{2,1,0:T(8,128)S(1)}, ...), condition=%wide.region_1.2_spmd, body=%wide.region_0.1_spmd.sunk | while | flops 851970 | bytes 2564349 | solution.py:77
  18.1 4.3 collective-permute-start
  22.4 1.3 collective-permute-start.1
  23.8 4.6 collective-permute-done.1
  28.4 1.4 collective-permute-start.2
  29.9 1.3 collective-permute-start.3
  31.2 3.6 collective-permute-done.3
  35.2 4.8 collective-permute-start
  40.1 1.3 collective-permute-start.1
  41.5 4.2 collective-permute-done.1
  45.7 2.9 collective-permute-start.2
  48.6 1.3 collective-permute-start.3
  49.9 2.7 collective-permute-done.3
  53.1 2.9 collective-permute-start
  56.1 1.3 collective-permute-start.1
  57.5 4.2 collective-permute-done.1
  61.7 3.2 collective-permute-start.2
  64.9 1.3 collective-permute-start.3
  66.2 2.4 collective-permute-done.3
  69.1 4.8 collective-permute-start
  73.9 1.3 collective-permute-start.1
  75.4 4.2 collective-permute-done.1
  79.6 2.9 collective-permute-start.2
  82.5 1.3 collective-permute-start.3
  83.8 2.7 collective-permute-done.3
  87.0 1.2 convolution_bitcast_fusion.2
  88.3 117.4 %all-reduce.5.cloned.1.call-done = f32[128,128]{0,1:T(8,128)} async-done(((f32[128,128]{0,1:T(8,128)}), f32[128,128]{0,1:T(8,128)}) %all-reduce.5.cloned.1.call-update) | async-done | bytes 65552 | tf_op jit(solution)/shard_map/psum | solution.py:78
  205.7 1.2 fusion.9
  206.9 1.2 convolution_bitcast_fusion.1
  208.2 122.0 %all-reduce.7.cloned.1.call-done = f32[128,128]{0,1:T(8,128)} async-done(((f32[128,128]{0,1:T(8,128)}), f32[128,128]{0,1:T(8,128)}) %all-reduce.7.cloned.1.call-update) | async-done | bytes 65552 | tf_op jit(solution)/shard_map/psum | solution.py:80
  330.2 0.8 broadcast_multiply_fusion.2
  331.1 0.7 copy-done.2
  331.9 11.7 %cholesky.16 = f32[128,128]{1,0:T(8,128)S(1)} custom-call(f32[128,128]{1,0:T(8,128)S(1)} %fusion.24), custom_call_target="Cholesky" | custom-call | tf_op jit(solution)/shard_map/jit(cholesky)/cholesky | solution.py:81
  345.0 9.8 %custom-call.6 = f32[1,128,128]{1,2,0:T(8,128)S(1)} custom-call(f32[1,128,128]{2,1,0:T(8,128)S(1)} %fusion.21), custom_call_target="InvertDiagBlocksLowerTriangular" | custom-call | tf_op jit(solution)/shard_map/triangular_solve | solution.py:83
  355.2 1.3 collective-permute-start.6
  356.5 4.5 collective-permute-start.7
  361.1 1.3 collective-permute-done.7
  362.5 1.3 collective-permute-start.8
  363.8 3.0 collective-permute-start.9
  366.8 1.3 fusion.10
  368.6 1.2 fusion.33
  369.8 127.4 %all-reduce.9.cloned.1.call-done = (f32[128,128]{0,1:T(8,128)}, f32[128,128]{0,1:T(8,128)}) async-done(((f32[128,128]{0,1:T(8,128)}, f32[128,128]{0,1:T(8,128)}), (f32[128,128]{0,1:T(8,128)}, f32[128,128]{0,1:T(8,128)})) %all-reduce.9.cloned.1.call-update) | async-done | bytes 131088 | tf_op jit(solution)/shard_map/psum | solution.py:89
  497.2 0.9 broadcast_multiply_fusion
  498.1 0.7 copy.14
  (82 shorter events, 7.3 us)
Async XLA Ops:
  7.2 0.7 copy-start.5
  7.2 198.5 %all-reduce.5.cloned.1.call-start = ((), (), s32[]{:S(2)}) async-start(), calls=%async_computation | async-start | bytes 131072 | tf_op jit(solution)/shard_map/psum | solution.py:78
  7.9 2.5 copy-start.4
  7.9 6.9 %collective-permute-start.5 = (f32[16,1]{1,0:T(8,128)S(1)}, f32[16,1]{1,0:T(8,128)S(1)}, u32[]{:S(2)}, u32[]{:S(2)}) collective-permute-start(f32[16,1]{1,0:T(8,128)S(1)} %slice.102), channel_id=1, source_target_pairs={{0,1},{1,2},{2,3},{4,5},{5,6},{6,7},{8,9},{9,10},{10,11},{12,13},{... | collective-permute-start | bytes 200 | tf_op jit(solution)/shard_map/ppermute | solution.py:16
  10.5 5.5 %collective-permute-start.4 = (f32[1,32]{1,0:T(1,128)S(1)}, f32[1,32]{1,0:T(1,128)S(1)}, u32[]{:S(2)}, u32[]{:S(2)}) collective-permute-start(f32[1,32]{1,0:T(1,128)S(1)} %slice.100), channel_id=1, source_target_pairs={{0,4},{4,8},{8,12},{12,16},{16,20},{20,24},{24,28},{1,5},{5,9},{9,... | collective-permute-start | bytes 392 | tf_op jit(solution)/shard_map/ppermute | solution.py:16
  14.8 1.3 copy-start.3
  14.8 1.3 copy-start.6
  16.1 0.7 copy-start.7
  18.0 69.0 %copy-start.1 = (f32[16,32,128]{2,1,0:T(8,128)S(1)}, f32[16,32,128]{2,1,0:T(8,128)}, u32[]{:S(2)}) copy-start(f32[16,32,128]{2,1,0:T(8,128)} %param.8) | copy-start | bytes 786436
  18.1 5.7 %collective-permute-start = (f32[1,32,128]{2,1,0:T(8,128)S(1)}, f32[1,32,128]{2,1,0:T(8,128)S(1)}, u32[]{:S(2)}, u32[]{:S(2)}) collective-permute-start(f32[1,32,128]{2,1,0:T(8,128)S(1)} %get-tuple-element.136), channel_id=1, source_target_pairs={{0,4},{4,8},{8,12},{12,16},{16,20},{20,24},{24,28},{1,5},{5,9},{9,... | collective-permute-start | bytes 49160 | tf_op jit(solution)/shard_map/while/body/eval_jaxpr/ppermute | solution.py:27
  22.4 6.1 %collective-permute-start.1 = (f32[1,32,128]{2,1,0:T(8,128)S(1)}, f32[1,32,128]{2,1,0:T(8,128)S(1)}, u32[]{:S(2)}, u32[]{:S(2)}) collective-permute-start(f32[1,32,128]{2,1,0:T(8,128)S(1)} %get-tuple-element.137), channel_id=1, source_target_pairs={{4,0},{8,4},{12,8},{16,12},{20,16},{24,20},{28,24},{5,1},{9,5},{13... | collective-permute-start | bytes 49160 | tf_op jit(solution)/shard_map/while/body/eval_jaxpr/ppermute | solution.py:29
  28.4 2.7 collective-permute-start.2
  29.9 4.9 collective-permute-start.3
  35.2 6.3 %collective-permute-start = (f32[1,32,128]{2,1,0:T(8,128)S(1)}, f32[1,32,128]{2,1,0:T(8,128)S(1)}, u32[]{:S(2)}, u32[]{:S(2)}) collective-permute-start(f32[1,32,128]{2,1,0:T(8,128)S(1)} %get-tuple-element.136), channel_id=1, source_target_pairs={{0,4},{4,8},{8,12},{12,16},{16,20},{20,24},{24,28},{1,5},{5,9},{9,... | collective-permute-start | bytes 49160 | tf_op jit(solution)/shard_map/while/body/eval_jaxpr/ppermute | solution.py:27
  40.1 5.6 %collective-permute-start.1 = (f32[1,32,128]{2,1,0:T(8,128)S(1)}, f32[1,32,128]{2,1,0:T(8,128)S(1)}, u32[]{:S(2)}, u32[]{:S(2)}) collective-permute-start(f32[1,32,128]{2,1,0:T(8,128)S(1)} %get-tuple-element.137), channel_id=1, source_target_pairs={{4,0},{8,4},{12,8},{16,12},{20,16},{24,20},{28,24},{5,1},{9,5},{13... | collective-permute-start | bytes 49160 | tf_op jit(solution)/shard_map/while/body/eval_jaxpr/ppermute | solution.py:29
  45.7 4.2 collective-permute-start.2
  48.6 4.0 collective-permute-start.3
  53.1 4.4 collective-permute-start
  56.1 5.6 %collective-permute-start.1 = (f32[1,32,128]{2,1,0:T(8,128)S(1)}, f32[1,32,128]{2,1,0:T(8,128)S(1)}, u32[]{:S(2)}, u32[]{:S(2)}) collective-permute-start(f32[1,32,128]{2,1,0:T(8,128)S(1)} %get-tuple-element.137), channel_id=1, source_target_pairs={{4,0},{8,4},{12,8},{16,12},{20,16},{24,20},{28,24},{5,1},{9,5},{13... | collective-permute-start | bytes 49160 | tf_op jit(solution)/shard_map/while/body/eval_jaxpr/ppermute | solution.py:29
  61.7 4.5 collective-permute-start.2
  64.9 3.8 collective-permute-start.3
  69.1 6.3 %collective-permute-start = (f32[1,32,128]{2,1,0:T(8,128)S(1)}, f32[1,32,128]{2,1,0:T(8,128)S(1)}, u32[]{:S(2)}, u32[]{:S(2)}) collective-permute-start(f32[1,32,128]{2,1,0:T(8,128)S(1)} %get-tuple-element.136), channel_id=1, source_target_pairs={{0,4},{4,8},{8,12},{12,16},{16,20},{20,24},{24,28},{1,5},{5,9},{9,... | collective-permute-start | bytes 49160 | tf_op jit(solution)/shard_map/while/body/eval_jaxpr/ppermute | solution.py:27
  73.9 5.6 %collective-permute-start.1 = (f32[1,32,128]{2,1,0:T(8,128)S(1)}, f32[1,32,128]{2,1,0:T(8,128)S(1)}, u32[]{:S(2)}, u32[]{:S(2)}) collective-permute-start(f32[1,32,128]{2,1,0:T(8,128)S(1)} %get-tuple-element.137), channel_id=1, source_target_pairs={{4,0},{8,4},{12,8},{16,12},{20,16},{24,20},{28,24},{5,1},{9,5},{13... | collective-permute-start | bytes 49160 | tf_op jit(solution)/shard_map/while/body/eval_jaxpr/ppermute | solution.py:29
  79.6 4.2 collective-permute-start.2
  82.5 4.0 collective-permute-start.3
  88.2 242.0 %all-reduce.7.cloned.1.call-start = ((), (), s32[]{:S(2)}) async-start(), calls=%async_computation.1 | async-start | bytes 131072 | tf_op jit(solution)/shard_map/psum | solution.py:80
  208.2 289.1 %all-reduce.9.cloned.1.call-start = ((), (), s32[]{:S(2)}) async-start(), calls=%async_computation.2 | async-start | bytes 262144 | tf_op jit(solution)/shard_map/psum | solution.py:89
  331.1 0.8 copy-start.2
  355.1 13.4 %copy-start = (f32[512,128]{1,0:T(8,128)}, f32[512,128]{1,0:T(8,128)S(1)}, u32[]{:S(2)}) copy-start(f32[512,128]{1,0:T(8,128)S(1)} %fusion.22) | copy-start | bytes 786436
  355.2 5.9 %collective-permute-start.6 = (f32[1,32,128]{2,1,0:T(8,128)S(1)}, f32[1,32,128]{2,1,0:T(8,128)S(1)}, u32[]{:S(2)}, u32[]{:S(2)}) collective-permute-start(f32[1,32,128]{2,1,0:T(8,128)S(1)} %get-tuple-element.80), channel_id=1, source_target_pairs={{4,0},{8,4},{12,8},{16,12},{20,16},{24,20},{28,24},{5,1},{9,5},{13... | collective-permute-start | bytes 49160 | tf_op jit(solution)/shard_map/ppermute | solution.py:29
  356.5 6.0 %collective-permute-start.7 = (f32[1,32,128]{2,1,0:T(8,128)S(1)}, f32[1,32,128]{2,1,0:T(8,128)S(1)}, u32[]{:S(2)}, u32[]{:S(2)}) collective-permute-start(f32[1,32,128]{2,1,0:T(8,128)S(1)} %get-tuple-element.79), channel_id=1, source_target_pairs={{0,4},{4,8},{8,12},{12,16},{16,20},{20,24},{24,28},{1,5},{5,9},{9,... | collective-permute-start | bytes 49160 | tf_op jit(solution)/shard_map/ppermute | solution.py:27
  362.5 5.7 %collective-permute-start.8 = (f32[18,1,128]{2,1,0:T(1,128)S(1)}, f32[18,1,128]{2,1,0:T(1,128)S(1)}, u32[]{:S(2)}, u32[]{:S(2)}) collective-permute-start(f32[18,1,128]{2,1,0:T(1,128)S(1)} %get-tuple-element.77), channel_id=1, source_target_pairs={{1,0},{2,1},{3,2},{5,4},{6,5},{7,6},{9,8},{10,9},{11,10},{13,12},{... | collective-permute-start | bytes 27656 | tf_op jit(solution)/shard_map/ppermute | solution.py:29
  363.8 4.4 collective-permute-start.9
Sparse Core Ops, SparseCore 0:
  88.3 117.3 all-reduce.4
  211.8 118.3 all-reduce.6
  369.9 127.2 all-reduce.8
where the time goes:
time: 507 us; the launch traced here: 506 us
  waiting for transfers between devices  399 us (79%)
  starting transfers between devices  54.5 us (11%)
  other arithmetic  28.1 us (6%)
  between operations  14 us (3%)
  matrix products  6.58 us (1%)
    psum x1, waiting for transfers between devices, per_device(): lax.psum((local_inner(new_basis, g_image), local_inner(new_basis, capacit...  127 us
    psum x1, waiting for transfers between devices, per_device(): gram = lax.psum(local_inner(cand, cand), ('gx', 'gy')) / nodes  122 us
    psum x1, waiting for transfers between devices, per_device(): proj = lax.psum(local_inner(prior_basis, field), ('gx', 'gy')) / nodes  117 us
    ppermute x10, starting transfers between devices, padded(): lax.ppermute(tail, axis, [(i, (i + 1) % count) for i in range(ends)])  34.8 us
    ppermute x10, waiting for transfers between devices, padded(): lax.ppermute(head, axis, [((i + 1) % count, i) for i in range(ends)])  28.7 us
    ppermute x10, starting transfers between devices, padded(): lax.ppermute(head, axis, [((i + 1) % count, i) for i in range(ends)])  12.9 us
    another operation x3, other arithmetic, per_device(): lower = jnp.linalg.cholesky(gram)  12.4 us
    another operation x2, other arithmetic, per_device(): lax.linalg.triangular_solve(lower, flat, left_side=False, lower=True, tra...  10.5 us
  transfers between devices with their start and end apart: 25, of which 17 were waited for; matrix products, arithmetic and copies ran while one was open for 0% of the time, Pallas kernels for 0%

commit v1 on v0

--- a/solution.py
+++ b/solution.py
@@ -75,7 +75,7 @@
         return (rhs + neighbors(ext, links)) / diag
 
     field = lax.fori_loop(0, SWEEPS, sweep, rhs / diag)
-    proj = lax.psum(local_inner(prior_basis, field), ("gx", "gy")) / nodes
+    proj = jnp.sum(lax.all_gather(local_inner(prior_basis, field), ("gx", "gy")), axis=0) / nodes
     cand = field - jnp.einsum("xyk,kp->xyp", prior_basis, proj, precision=highest)
     gram = lax.psum(local_inner(cand, cand), ("gx", "gy")) / nodes
     lower = jnp.linalg.cholesky(gram)

time: 507 us -> 445 us (0.88)
  waiting for transfers between devices: 399 us -> 334 us
    psum x1 -> x0, waiting for transfers between devices: 117 us -> none  [per_device(): proj = lax.psum(local_inner(prior_basis, field), ('gx', 'gy')) / nodes]
    all_gather x0 -> x1, waiting for transfers between devices: none -> 56.5 us  [per_device(): lax.all_gather(local_inner(prior_basis, field), ('gx', 'gy'))]
  transfers between devices with their start and end apart: 25 -> 25, of which waited for: 17 -> 17; matrix products, arithmetic and copies ran while one was open for 0% -> 1% of each run, Pallas kernels for 0% -> 0%
where the time goes in v1:
time: 445 us; the launch traced here: 444 us
  waiting for transfers between devices  334 us (75%)
  starting transfers between devices  54.4 us (12%)
  other arithmetic  31.4 us (7%)
  between operations  14 us (3%)
  matrix products  5.74 us (1%)
    psum x1, waiting for transfers between devices, per_device(): lax.psum((local_inner(new_basis, g_image), local_inner(new_basis, capacit...  127 us
    psum x1, waiting for transfers between devices, per_device(): gram = lax.psum(local_inner(cand, cand), ('gx', 'gy')) / nodes  119 us
    all_gather x1, waiting for transfers between devices, per_device(): lax.all_gather(local_inner(prior_basis, field), ('gx', 'gy'))  56.5 us
    ppermute x10, starting transfers between devices, padded(): lax.ppermute(tail, axis, [(i, (i + 1) % count) for i in range(ends)])  34.8 us
    ppermute x10, waiting for transfers between devices, padded(): lax.ppermute(head, axis, [((i + 1) % count, i) for i in range(ends)])  28.7 us
    ppermute x10, starting transfers between devices, padded(): lax.ppermute(head, axis, [((i + 1) % count, i) for i in range(ends)])  12.9 us
    another operation x3, other arithmetic, per_device(): lower = jnp.linalg.cholesky(gram)  12.4 us
    another operation x2, other arithmetic, per_device(): lax.linalg.triangular_solve(lower, flat, left_side=False, lower=True, tra...  10.5 us
  transfers between devices with their start and end apart: 25, of which 17 were waited for; matrix products, arithmetic and copies ran while one was open for 1% of the time, Pallas kernels for 0%

profile of v1, /device:TPU:0, one launch (start us, length us, event | category | flops | bytes accessed | tf_op | source)
XLA Modules:
  0.0 444.2 jit_solution(8457881702478309451)
XLA Ops:
  8.0 2.3 collective-permute-start.5
  11.2 4.2 collective-permute-start.4
  15.5 1.2 collective-permute-done.4
  16.7 0.8 multiply_add_fusion
  17.5 1.2 broadcast_divide_fusion
  18.7 69.0 %while.10 = (s32[]{:T(128)}, f32[16,32,128]{2,1,0:T(8,128)S(1)}, f32[16,32]{1,0:T(8,128)S(1)}, f32[16,32]{1,0:T(8,128)S(1)}, f32[16,32]{1,0:T(8,128)S(1)}, /*ind...) while((s32[]{:T(128)}, f32[16,32,128]{2,1,0:T(8,128)S(1)}, ...), condition=%wide.region_1.2_spmd, body=%wide.region_0.1_spmd.sunk | while | flops 851970 | bytes 2564349 | solution.py:77
  18.8 4.3 collective-permute-start
  23.1 1.3 collective-permute-start.1
  24.5 4.6 %collective-permute-done.1 = f32[1,32,128]{2,1,0:T(8,128)S(1)} collective-permute-done((f32[1,32,128]{2,1,0:T(8,128)S(1)}, f32[1,32,128]{2,1,0:T(8,128)S(1)}, u32[]{:S(2)}, u32[]{:S(2)}) %collective-permute-start.1) | collective-permute-done | bytes 16416 | tf_op jit(solution)/shard_map/while/body/eval_jaxpr/ppermute | solution.py:29
  29.2 1.4 collective-permute-start.2
  30.6 1.3 collective-permute-start.3
  31.9 3.6 collective-permute-done.3
  35.9 4.8 %collective-permute-start = (f32[1,32,128]{2,1,0:T(8,128)S(1)}, f32[1,32,128]{2,1,0:T(8,128)S(1)}, u32[]{:S(2)}, u32[]{:S(2)}) collective-permute-start(f32[1,32,128]{2,1,0:T(8,128)S(1)} %get-tuple-element.136), channel_id=1, source_target_pairs={{0,4},{4,8},{8,12},{12,16},{16,20},{20,24},{24,28},{1,5},{5,9},{9,... | collective-permute-start | bytes 49160 | tf_op jit(solution)/shard_map/while/body/eval_jaxpr/ppermute | solution.py:27
  40.8 1.3 collective-permute-start.1
  42.2 4.2 collective-permute-done.1
  46.4 2.9 collective-permute-start.2
  49.3 1.3 collective-permute-start.3
  50.6 2.7 collective-permute-done.3
  53.8 2.9 collective-permute-start
  56.8 1.3 collective-permute-start.1
  58.2 4.2 collective-permute-done.1
  62.4 3.2 collective-permute-start.2
  65.6 1.3 collective-permute-start.3
  66.9 2.4 collective-permute-done.3
  69.8 4.8 %collective-permute-start = (f32[1,32,128]{2,1,0:T(8,128)S(1)}, f32[1,32,128]{2,1,0:T(8,128)S(1)}, u32[]{:S(2)}, u32[]{:S(2)}) collective-permute-start(f32[1,32,128]{2,1,0:T(8,128)S(1)} %get-tuple-element.136), channel_id=1, source_target_pairs={{0,4},{4,8},{8,12},{12,16},{16,20},{20,24},{24,28},{1,5},{5,9},{9,... | collective-permute-start | bytes 49160 | tf_op jit(solution)/shard_map/while/body/eval_jaxpr/ppermute | solution.py:27
  74.7 1.3 collective-permute-start.1
  76.1 4.2 collective-permute-done.1
  80.3 2.9 collective-permute-start.2
  83.2 1.3 collective-permute-start.3
  84.5 2.7 collective-permute-done.3
  87.7 1.2 convolution_bitcast_fusion.2
  89.0 56.5 %all-gather.3.cloned.1.call-done = f32[4096,128]{0,1:T(8,128)} async-done(((f32[128,128]{0,1:T(8,128)}), f32[4096,128]{0,1:T(8,128)}) %all-gather.3.cloned.1.call-update) | async-done | bytes 2097168 | tf_op jit(solution)/shard_map/all_gather | solution.py:78
  145.5 2.0 copy.22
  148.1 1.2 convolution_bitcast_fusion.1
  149.4 118.7 %all-reduce.4.cloned.1.call-done = f32[128,128]{0,1:T(8,128)} async-done(((f32[128,128]{0,1:T(8,128)}), f32[128,128]{0,1:T(8,128)}) %all-reduce.4.cloned.1.call-update) | async-done | bytes 65552 | tf_op jit(solution)/shard_map/psum | solution.py:80
  268.1 0.8 broadcast_multiply_fusion.2
  269.1 0.9 fusion.24
  269.9 11.7 %cholesky.16 = f32[128,128]{1,0:T(8,128)S(1)} custom-call(f32[128,128]{1,0:T(8,128)S(1)} %fusion.24), custom_call_target="Cholesky" | custom-call | tf_op jit(solution)/shard_map/jit(cholesky)/cholesky | solution.py:81
  283.0 9.8 %custom-call.6 = f32[1,128,128]{1,2,0:T(8,128)S(1)} custom-call(f32[1,128,128]{2,1,0:T(8,128)S(1)} %fusion.21), custom_call_target="InvertDiagBlocksLowerTriangular" | custom-call | tf_op jit(solution)/shard_map/triangular_solve | solution.py:83
  293.2 1.3 collective-permute-start.6
  294.5 4.5 %collective-permute-start.7 = (f32[1,32,128]{2,1,0:T(8,128)S(1)}, f32[1,32,128]{2,1,0:T(8,128)S(1)}, u32[]{:S(2)}, u32[]{:S(2)}) collective-permute-start(f32[1,32,128]{2,1,0:T(8,128)S(1)} %get-tuple-element.79), channel_id=1, source_target_pairs={{0,4},{4,8},{8,12},{12,16},{16,20},{20,24},{24,28},{1,5},{5,9},{9,... | collective-permute-start | bytes 49160 | tf_op jit(solution)/shard_map/ppermute | solution.py:27
  299.2 1.3 collective-permute-done.7
  300.5 1.3 collective-permute-start.8
  301.8 3.0 collective-permute-start.9
  304.8 1.3 fusion.10
  306.6 1.2 fusion.33
  307.8 127.5 %all-reduce.6.cloned.1.call-done = (f32[128,128]{0,1:T(8,128)}, f32[128,128]{0,1:T(8,128)}) async-done(((f32[128,128]{0,1:T(8,128)}, f32[128,128]{0,1:T(8,128)}), (f32[128,128]{0,1:T(8,128)}, f32[128,128]{0,1:T(8,128)})) %all-reduce.6.cloned.1.call-update) | async-done | bytes 131088 | tf_op jit(solution)/shard_map/psum | solution.py:89
  435.3 0.9 broadcast_multiply_fusion
  (74 shorter events, 8.6 us)
Async XLA Ops:
  7.2 138.4 %all-gather.3.cloned.1.call-start = ((), (), s32[]{:S(2)}) async-start(), calls=%async_computation.1 | async-start | bytes 2162688 | tf_op jit(solution)/shard_map/all_gather | solution.py:78
  8.0 7.5 %collective-permute-start.5 = (f32[16,1]{1,0:T(8,128)S(1)}, f32[16,1]{1,0:T(8,128)S(1)}, u32[]{:S(2)}, u32[]{:S(2)}) collective-permute-start(f32[16,1]{1,0:T(8,128)S(1)} %slice.102), channel_id=1, source_target_pairs={{0,1},{1,2},{2,3},{4,5},{5,6},{6,7},{8,9},{9,10},{10,11},{12,13},{... | collective-permute-start | bytes 200 | tf_op jit(solution)/shard_map/ppermute | solution.py:16
  11.2 5.5 %collective-permute-start.4 = (f32[1,32]{1,0:T(1,128)S(1)}, f32[1,32]{1,0:T(1,128)S(1)}, u32[]{:S(2)}, u32[]{:S(2)}) collective-permute-start(f32[1,32]{1,0:T(1,128)S(1)} %slice.100), channel_id=1, source_target_pairs={{0,4},{4,8},{8,12},{12,16},{16,20},{20,24},{24,28},{1,5},{5,9},{9,... | collective-permute-start | bytes 392 | tf_op jit(solution)/shard_map/ppermute | solution.py:16
  18.7 69.0 %copy-start.1 = (f32[16,32,128]{2,1,0:T(8,128)S(1)}, f32[16,32,128]{2,1,0:T(8,128)}, u32[]{:S(2)}) copy-start(f32[16,32,128]{2,1,0:T(8,128)} %param.8) | copy-start | bytes 786436
  18.8 5.7 %collective-permute-start = (f32[1,32,128]{2,1,0:T(8,128)S(1)}, f32[1,32,128]{2,1,0:T(8,128)S(1)}, u32[]{:S(2)}, u32[]{:S(2)}) collective-permute-start(f32[1,32,128]{2,1,0:T(8,128)S(1)} %get-tuple-element.136), channel_id=1, source_target_pairs={{0,4},{4,8},{8,12},{12,16},{16,20},{20,24},{24,28},{1,5},{5,9},{9,... | collective-permute-start | bytes 49160 | tf_op jit(solution)/shard_map/while/body/eval_jaxpr/ppermute | solution.py:27
  23.1 6.1 %collective-permute-start.1 = (f32[1,32,128]{2,1,0:T(8,128)S(1)}, f32[1,32,128]{2,1,0:T(8,128)S(1)}, u32[]{:S(2)}, u32[]{:S(2)}) collective-permute-start(f32[1,32,128]{2,1,0:T(8,128)S(1)} %get-tuple-element.137), channel_id=1, source_target_pairs={{4,0},{8,4},{12,8},{16,12},{20,16},{24,20},{28,24},{5,1},{9,5},{13... | collective-permute-start | bytes 49160 | tf_op jit(solution)/shard_map/while/body/eval_jaxpr/ppermute | solution.py:29
  29.2 2.7 collective-permute-start.2
  30.6 4.9 %collective-permute-start.3 = (f32[18,1,128]{2,1,0:T(1,128)S(1)}, f32[18,1,128]{2,1,0:T(1,128)S(1)}, u32[]{:S(2)}, u32[]{:S(2)}) collective-permute-start(f32[18,1,128]{2,1,0:T(1,128)S(1)} %get-tuple-element.139), channel_id=1, source_target_pairs={{1,0},{2,1},{3,2},{5,4},{6,5},{7,6},{9,8},{10,9},{11,10},{13,12},{... | collective-permute-start | bytes 27656 | tf_op jit(solution)/shard_map/while/body/eval_jaxpr/ppermute | solution.py:29
  35.9 6.3 %collective-permute-start = (f32[1,32,128]{2,1,0:T(8,128)S(1)}, f32[1,32,128]{2,1,0:T(8,128)S(1)}, u32[]{:S(2)}, u32[]{:S(2)}) collective-permute-start(f32[1,32,128]{2,1,0:T(8,128)S(1)} %get-tuple-element.136), channel_id=1, source_target_pairs={{0,4},{4,8},{8,12},{12,16},{16,20},{20,24},{24,28},{1,5},{5,9},{9,... | collective-permute-start | bytes 49160 | tf_op jit(solution)/shard_map/while/body/eval_jaxpr/ppermute | solution.py:27
  40.8 5.6 %collective-permute-start.1 = (f32[1,32,128]{2,1,0:T(8,128)S(1)}, f32[1,32,128]{2,1,0:T(8,128)S(1)}, u32[]{:S(2)}, u32[]{:S(2)}) collective-permute-start(f32[1,32,128]{2,1,0:T(8,128)S(1)} %get-tuple-element.137), channel_id=1, source_target_pairs={{4,0},{8,4},{12,8},{16,12},{20,16},{24,20},{28,24},{5,1},{9,5},{13... | collective-permute-start | bytes 49160 | tf_op jit(solution)/shard_map/while/body/eval_jaxpr/ppermute | solution.py:29
  46.4 4.2 collective-permute-start.2
  49.3 4.0 collective-permute-start.3
  53.8 4.4 collective-permute-start
  56.8 5.6 %collective-permute-start.1 = (f32[1,32,128]{2,1,0:T(8,128)S(1)}, f32[1,32,128]{2,1,0:T(8,128)S(1)}, u32[]{:S(2)}, u32[]{:S(2)}) collective-permute-start(f32[1,32,128]{2,1,0:T(8,128)S(1)} %get-tuple-element.137), channel_id=1, source_target_pairs={{4,0},{8,4},{12,8},{16,12},{20,16},{24,20},{28,24},{5,1},{9,5},{13... | collective-permute-start | bytes 49160 | tf_op jit(solution)/shard_map/while/body/eval_jaxpr/ppermute | solution.py:29
  62.4 4.5 %collective-permute-start.2 = (f32[18,1,128]{2,1,0:T(1,128)S(1)}, f32[18,1,128]{2,1,0:T(1,128)S(1)}, u32[]{:S(2)}, u32[]{:S(2)}) collective-permute-start(f32[18,1,128]{2,1,0:T(1,128)S(1)} %get-tuple-element.138), channel_id=1, source_target_pairs={{0,1},{1,2},{2,3},{4,5},{5,6},{6,7},{8,9},{9,10},{10,11},{12,13},{... | collective-permute-start | bytes 27656 | tf_op jit(solution)/shard_map/while/body/eval_jaxpr/ppermute | solution.py:27
  65.6 3.8 collective-permute-start.3
  69.8 6.3 %collective-permute-start = (f32[1,32,128]{2,1,0:T(8,128)S(1)}, f32[1,32,128]{2,1,0:T(8,128)S(1)}, u32[]{:S(2)}, u32[]{:S(2)}) collective-permute-start(f32[1,32,128]{2,1,0:T(8,128)S(1)} %get-tuple-element.136), channel_id=1, source_target_pairs={{0,4},{4,8},{8,12},{12,16},{16,20},{20,24},{24,28},{1,5},{5,9},{9,... | collective-permute-start | bytes 49160 | tf_op jit(solution)/shard_map/while/body/eval_jaxpr/ppermute | solution.py:27
  74.7 5.6 %collective-permute-start.1 = (f32[1,32,128]{2,1,0:T(8,128)S(1)}, f32[1,32,128]{2,1,0:T(8,128)S(1)}, u32[]{:S(2)}, u32[]{:S(2)}) collective-permute-start(f32[1,32,128]{2,1,0:T(8,128)S(1)} %get-tuple-element.137), channel_id=1, source_target_pairs={{4,0},{8,4},{12,8},{16,12},{20,16},{24,20},{28,24},{5,1},{9,5},{13... | collective-permute-start | bytes 49160 | tf_op jit(solution)/shard_map/while/body/eval_jaxpr/ppermute | solution.py:29
  80.3 4.2 collective-permute-start.2
  83.2 4.0 collective-permute-start.3
  88.9 179.2 %all-reduce.4.cloned.1.call-start = ((), (), s32[]{:S(2)}) async-start(), calls=%async_computation | async-start | bytes 131072 | tf_op jit(solution)/shard_map/psum | solution.py:80
  147.5 151.6 %copy-start.2 = (f32[16,32]{1,0:T(8,128)S(1)}, f32[16,32]{1,0:T(8,128)}, u32[]{:S(2)}) copy-start(f32[16,32]{1,0:T(8,128)} %param.11) | copy-start | bytes 6148
  149.4 285.9 %all-reduce.6.cloned.1.call-start = ((), (), s32[]{:S(2)}) async-start(), calls=%async_computation.2 | async-start | bytes 262144 | tf_op jit(solution)/shard_map/psum | solution.py:89
  293.2 144.5 %copy-start = (f32[512,128]{1,0:T(8,128)}, f32[512,128]{1,0:T(8,128)S(1)}, u32[]{:S(2)}) copy-start(f32[512,128]{1,0:T(8,128)S(1)} %fusion.22) | copy-start | bytes 786436
  293.2 5.9 %collective-permute-start.6 = (f32[1,32,128]{2,1,0:T(8,128)S(1)}, f32[1,32,128]{2,1,0:T(8,128)S(1)}, u32[]{:S(2)}, u32[]{:S(2)}) collective-permute-start(f32[1,32,128]{2,1,0:T(8,128)S(1)} %get-tuple-element.80), channel_id=1, source_target_pairs={{4,0},{8,4},{12,8},{16,12},{20,16},{24,20},{28,24},{5,1},{9,5},{13... | collective-permute-start | bytes 49160 | tf_op jit(solution)/shard_map/ppermute | solution.py:29
  294.5 6.0 %collective-permute-start.7 = (f32[1,32,128]{2,1,0:T(8,128)S(1)}, f32[1,32,128]{2,1,0:T(8,128)S(1)}, u32[]{:S(2)}, u32[]{:S(2)}) collective-permute-start(f32[1,32,128]{2,1,0:T(8,128)S(1)} %get-tuple-element.79), channel_id=1, source_target_pairs={{0,4},{4,8},{8,12},{12,16},{16,20},{20,24},{24,28},{1,5},{5,9},{9,... | collective-permute-start | bytes 49160 | tf_op jit(solution)/shard_map/ppermute | solution.py:27
  300.5 5.7 %collective-permute-start.8 = (f32[18,1,128]{2,1,0:T(1,128)S(1)}, f32[18,1,128]{2,1,0:T(1,128)S(1)}, u32[]{:S(2)}, u32[]{:S(2)}) collective-permute-start(f32[18,1,128]{2,1,0:T(1,128)S(1)} %get-tuple-element.77), channel_id=1, source_target_pairs={{1,0},{2,1},{3,2},{5,4},{6,5},{7,6},{9,8},{10,9},{11,10},{13,12},{... | collective-permute-start | bytes 27656 | tf_op jit(solution)/shard_map/ppermute | solution.py:29
  301.8 4.4 collective-permute-start.9
Sparse Core Ops, SparseCore 0:
  89.1 56.4 all-gather.2
  151.7 116.4 all-reduce.3
  308.0 127.2 all-reduce.5
